TPU v7x, 128 devices: a whole 4x4x4 slice. The times are simulated.
128 devices in a mesh: req: 8 (over y, x_hi), row: 4 (over x_lo, core), col: 4 (over z).
Axes of the slice: x: 4 (x_hi: 2, x_lo: 2; x = x_hi * 2 + x_lo), y: 4, z: 4, core: 2. Of those that a mesh axis runs over, the one named last changes fastest.
Arguments:
- text_embed: bfloat16 [6144, 4096], P(('req', 'col'), 'row')
- vis_embed: bfloat16 [4096, 4096], P(('req', 'col'), 'row')
- vis_segment: int32 [4096], P(('req', 'col')), may hold values from 0 to 20, never falling along the last dimension, each value on 1 to 256 neighbouring positions
- vis_valid: int32 [4096], P(('req', 'col')), may hold values 0 or 1
- vis_gain: bfloat16 [4096], P('row'), may hold values from 0.25 to 1.75
- vis_wq: bfloat16 [4096, 4096], P('row', 'col')
- vis_wk: bfloat16 [4096, 4096], P('row', 'col')
- vis_wv: bfloat16 [4096, 4096], P('row', 'col'), may hold values from -0.09375 to 0.09375
- vis_wo: bfloat16 [4096, 4096], P('col', 'row'), may hold values from -0.09375 to 0.09375
- dec_gain: bfloat16 [4096], P('row'), may hold values from 0.25 to 1.75
- dec_wq: bfloat16 [4096, 4096], P('row', 'col')
- dec_wk: bfloat16 [4096, 4096], P('row', 'col')
- dec_wv: bfloat16 [4096, 4096], P('row', 'col'), may hold values from -0.09375 to 0.09375
- dec_wo: bfloat16 [4096, 4096], P('col', 'row'), may hold values from -0.09375 to 0.09375
Outputs:
- hidden_out: bfloat16 [6144, 4096], P(('req', 'col'), 'row')
Inputs may be any that keep to these rules, and one draw needn't show every extreme that they name: `vis_segment`: images take consecutive slots in order, each 1 to 256 slots, one exactly 256.
All inputs are finite; a program needn't handle non-finite values. No bound on the sum of `vis_valid` on one device may be relied on, other than what follows from the above.
Results may differ from a plain program's by a relative error of at most 0.008.
Values may be sent and summed in bfloat16 or wider, within the bound.
No kernel may reach another device: no remote copies, remote signals or barrier semaphores. Data moves between devices by JAX's collectives and lax.ppermute only.
A program may use at most 192 MiB of HBM per device.

v0:
```python
import jax
import jax.numpy as jnp
from jax import lax
from jax.sharding import PartitionSpec as P

D = 4096
HD = 128
MAXIMG = 256


def with_halo(cells, sides, width):
    for axis, dim in sides:
        count = lax.axis_size(axis)
        ends = count - 1
        head = lax.slice_in_dim(cells, 0, width, axis=dim)
        tail = lax.slice_in_dim(cells, cells.shape[dim] - width, cells.shape[dim], axis=dim)
        cells = jnp.concatenate(
            [
                lax.ppermute(tail, axis, [(i, (i + 1) % count) for i in range(ends)]),
                cells,
                lax.ppermute(head, axis, [((i + 1) % count, i) for i in range(ends)]),
            ],
            axis=dim,
        )
    return cells


def passed_along(shard, axis, by):
    size = lax.axis_size(axis)
    pairs = [(i, i + by) for i in range(size) if 0 <= i + by < size]
    return lax.ppermute(shard, axis, pairs)


def norm_local(values, gain):
    floats = values.astype(jnp.float32)
    squares = jnp.sum(floats * floats, axis=-1)
    totals = lax.psum(squares, "row")
    factor = lax.rsqrt(totals / D + 1e-05)
    return (floats * factor[:, None] * gain.astype(jnp.float32)[None, :]).astype(jnp.bfloat16)


def gather_cols(values):
    return lax.all_gather(values, "col", axis=0, tiled=True)


def out_project(attended, weight):
    whole = lax.all_gather(attended, "row", axis=0, tiled=True)
    return lax.psum_scatter(
        jnp.dot(whole, weight, preferred_element_type=jnp.float32).astype(jnp.bfloat16),
        "col",
        scatter_dimension=0,
        tiled=True,
    ).astype(jnp.float32)


def split_heads(values):
    return values.reshape(values.shape[0], values.shape[1] // HD, HD)


def attend_block(queries, keys, values, allowed):
    query_heads = split_heads(queries)
    scores = jnp.einsum(
        "qhd,khd->hqk", query_heads, split_heads(keys), preferred_element_type=jnp.float32
    ) * HD ** (-0.5)
    scores = jnp.where(allowed[None], scores, -1e30)
    peak = jnp.max(scores, axis=-1, keepdims=True)
    weights = jnp.where(allowed[None], jnp.exp(scores - peak), 0.0)
    mass = jnp.sum(weights, axis=-1)
    summed = jnp.einsum(
        "hqk,khd->qhd",
        weights.astype(jnp.bfloat16),
        split_heads(values),
        preferred_element_type=jnp.float32,
    )
    result = summed / jnp.transpose(mass)[:, :, None]
    return result.reshape(queries.shape[0], queries.shape[1]).astype(jnp.bfloat16)


def fold_step(carry, query_heads, query_slots, key_heads, value_heads):
    peak, mass, accum = carry
    piece_slots = jnp.arange(key_heads.shape[0], dtype=jnp.int32)
    allowed = query_slots[:, None] >= piece_slots[None, :]
    scores = jnp.einsum(
        "qhd,khd->hqk", query_heads, key_heads, preferred_element_type=jnp.float32
    ) * HD ** (-0.5)
    scores = jnp.where(allowed[None], scores, -1e30)
    new_peak = jnp.maximum(peak, jnp.max(scores, axis=-1))
    weights = jnp.where(allowed[None], jnp.exp(scores - new_peak[:, :, None]), 0.0)
    summed = jnp.einsum(
        "hqk,khd->hqd",
        weights.astype(jnp.bfloat16),
        value_heads,
        preferred_element_type=jnp.float32,
    )
    return (new_peak, jnp.sum(weights, axis=-1), summed)


def start_state(head_count, query_count):
    return (
        jnp.full((head_count, query_count), -1e30, jnp.float32),
        jnp.zeros((head_count, query_count), jnp.float32),
        jnp.zeros((head_count, query_count, HD), jnp.float32),
    )


def head_project(values, weights):
    row_count = lax.axis_size("row")
    width = weights[0].shape[1]
    depth = weights[0].shape[0]
    shaped = jnp.stack(
        [w.reshape(depth, row_count, width // row_count) for w in weights], axis=2
    ).reshape(depth, row_count, len(weights) * (width // row_count))
    summed = jnp.einsum("tf,frc->rtc", values, shaped, preferred_element_type=jnp.float32)
    summed = summed.astype(jnp.bfloat16).reshape(row_count * values.shape[0], -1)
    return lax.psum_scatter(summed, "row", scatter_dimension=0, tiled=True)


def out_project_heads(attended, weight):
    row_count = lax.axis_size("row")
    whole = lax.all_gather(attended, "row", axis=0, tiled=False)
    shaped = weight.reshape(row_count, weight.shape[0] // row_count, weight.shape[1])
    summed = jnp.einsum("rtf,rfo->to", whole, shaped, preferred_element_type=jnp.float32)
    return lax.psum_scatter(
        summed.astype(jnp.bfloat16), "col", scatter_dimension=0, tiled=True
    ).astype(jnp.float32)


def per_device(
    text_embed,
    vis_embed,
    vis_segment,
    vis_valid,
    vis_gain,
    vis_wq,
    vis_wk,
    vis_wv,
    vis_wo,
    dec_gain,
    dec_wq,
    dec_wk,
    dec_wv,
    dec_wo,
):
    row_count = lax.axis_size("row")
    col_count = lax.axis_size("col")
    width = vis_wq.shape[1]
    local = width // row_count
    margin = MAXIMG - 1
    piece_ids = lax.all_gather(jnp.stack([vis_segment, vis_valid]), "col", axis=1, tiled=True)
    piece_len = piece_ids.shape[1]
    framed_ids = with_halo(piece_ids, (("req", 1),), margin)
    total_slots = piece_len * lax.axis_size("req")
    prompt_rows = text_embed.shape[0]
    prompt_total = prompt_rows * lax.axis_size("req") * col_count
    window_len = piece_len + 2 * margin
    window_start = lax.axis_index("req") * piece_len - margin
    window_index = jnp.arange(window_len, dtype=jnp.int32)
    key_slots = window_start + window_index
    inside = (key_slots >= 0) & (key_slots < total_slots)
    key_segment = framed_ids[0]
    key_valid = framed_ids[1]
    begins = jnp.concatenate([jnp.ones((1,), jnp.bool_), key_segment[1:] != key_segment[:-1]])
    begins = begins | (key_slots == 0)
    image_first = lax.cummax(jnp.where(begins, key_slots, window_start), axis=0)
    target_window = image_first * prompt_total // total_slots + key_slots - image_first
    vis_cols = gather_cols(norm_local(vis_embed, vis_gain))
    vis_proj = head_project(vis_cols, (vis_wq, vis_wk, vis_wv))
    vis_pairs = jnp.stack([vis_proj[:, local : 2 * local], vis_proj[:, 2 * local :]])
    framed = with_halo(vis_pairs, (("req", 1),), margin)
    query_local = margin + jnp.arange(piece_len, dtype=jnp.int32)
    query_slots = window_start + query_local
    query_segment = key_segment[query_local]
    seen = (
        inside[None, :]
        & (query_segment[:, None] == key_segment[None, :])
        & ((key_valid[None, :] == 1) | (query_slots[:, None] == key_slots[None, :]))
    )
    vis_att = attend_block(vis_proj[:, :local], framed[0], framed[1], seen)
    vis_out = (vis_embed.astype(jnp.float32) + out_project_heads(vis_att, vis_wo)).astype(
        jnp.bfloat16
    )
    device_place = lax.axis_index("req") * col_count + lax.axis_index("col")
    owned = device_place * prompt_rows + jnp.arange(prompt_rows, dtype=jnp.int32)
    slot_rows = vis_out.shape[0]
    following = passed_along(vis_out, ("req", "col"), -1)
    near_rows = jnp.concatenate([vis_out, following], axis=0)
    near_local = (
        margin + lax.axis_index("col") * slot_rows + jnp.arange(2 * slot_rows, dtype=jnp.int32)
    )
    near_slots = window_start + near_local
    present = near_slots < total_slots
    near_target = jnp.where(present, target_window[near_local], -1)
    near_valid = key_valid[near_local]
    onehot = ((owned[:, None] == near_target[None, :]) & (near_valid[None, :] == 1)).astype(
        jnp.bfloat16
    )
    carried = jnp.dot(onehot, near_rows, preferred_element_type=jnp.float32)
    mixed = (text_embed.astype(jnp.float32) + carried).astype(jnp.bfloat16)
    dec_cols = gather_cols(norm_local(mixed, dec_gain))
    dec_proj = head_project(dec_cols, (dec_wq, dec_wk, dec_wv))
    dec_rows = dec_cols.shape[0]
    dec_pairs = jnp.stack([dec_proj[:, local : 2 * local], dec_proj[:, 2 * local :]])
    piece = lax.all_gather(dec_pairs, "req", axis=1, tiled=True)
    token_slots = lax.axis_index("req") * dec_rows + jnp.arange(dec_rows, dtype=jnp.int32)
    all_slots = jnp.arange(piece.shape[1], dtype=jnp.int32)
    causal = token_slots[:, None] >= all_slots[None, :]
    dec_att = attend_block(dec_proj[:, :local], piece[0], piece[1], causal)
    return (mixed.astype(jnp.float32) + out_project_heads(dec_att, dec_wo)).astype(jnp.bfloat16)


def solution(mesh):
    return jax.shard_map(
        per_device,
        mesh=mesh,
        in_specs=(
            P(("req", "col"), "row"),
            P(("req", "col"), "row"),
            P(("req", "col")),
            P(("req", "col")),
            P("row"),
            P("row", "col"),
            P("row", "col"),
            P("row", "col"),
            P("col", "row"),
            P("row"),
            P("row", "col"),
            P("row", "col"),
            P("row", "col"),
            P("col", "row"),
        ),
        out_specs=P(("req", "col"), "row"),
        check_vma=False,
    )
```

profile of v0, /device:TPU:0, one launch (start us, length us, event | category | flops | bytes accessed | tf_op | source)
XLA Modules:
  0.0 511.5 jit_solution(722304668159904372)
XLA Ops:
  7.8 7.0 %psum.14 = f32[128]{0:T(128)S(1)} all-reduce(f32[128]{0:T(128)S(1)} %fusion.36), channel_id=1, replica_groups=mesh['req'=8,'row'=4,'col'=4] {'row'}, use_global_device_ids=true, to_apply=%region_3.4 | all-reduce | flops 128 | bytes 1024 | tf_op jit(solution)/shard_map/psum | solution.py:37
  29.2 6.6 %pad_maximum_fusion = bf16[1024,4,3,256]{0,3,2,1:T(8,128)(2,1)} fusion(bf16[1024,4,1,256]{0,3,2,1:T(8,128)(2,1)} %bitcast.89, bf16[1024,4,1,256]{0,3,2,1:T(8,128)(2,1)} %bitcast.88, bf16[1024,4,1,256]{0,3,2,1:T(8,128)(2,1)} %bitcast.87), kind=kLoop, calls=%fused_computation.14 | loop fusion | flops 6291456 | bytes 12582912 | tf_op jit(solution)/shard_map/stack | solution.py:110
  35.7 7.9 %all-gather.6.cloned.1.call-done = bf16[512,1024]{1,0:T(8,128)(2,1)} async-done(((bf16[128,1024]{1,0:T(8,128)(2,1)}), bf16[512,1024]{1,0:T(8,128)(2,1)}) %all-gather.6.cloned.1.call-update) | async-done | bytes 1048592 | tf_op jit(solution)/shard_map/all_gather | solution.py:43
  43.7 8.2 %convolution_convert_fusion.1 = bf16[4,768,512]{1,2,0:T(8,128)(2,1)} fusion(bf16[1024,4,768]{0,2,1:T(8,128)(2,1)} %bitcast.93, bf16[512,1024]{1,0:T(8,128)(2,1)} %all-gather.6.cloned.1.call-done), kind=kOutput, calls=%fused_computation.21 | convolution fusion | flops 3222798336 | bytes 10485760 | tf_op jit(solution)/shard_map/tf,frc->rtc/dot_general | solution.py:113
  57.2 8.6 %all_gather.20 = s32[2,512]{1,0:T(2,128)S(1)} all-gather(s32[2,128]{1,0:T(2,128)S(1)} %pad_add_fusion.1), channel_id=1, replica_groups=mesh['req'=8,'row'=4,'col'=4] {'col'}, dimensions={1}, use_global_device_ids=true | all-gather | bytes 5120 | tf_op jit(solution)/shard_map/all_gather | solution.py:149
  72.1 5.6 %collective-permute-done.1 = s32[2,255]{1,0:T(2,128)S(1)} collective-permute-done((s32[2,255]{1,0:T(2,128)S(1)}, s32[2,255]{1,0:T(2,128)S(1)}, u32[]{:S(2)}, u32[]{:S(2)}) %collective-permute-start.1) | collective-permute-done | bytes 2072 | tf_op jit(solution)/shard_map/ppermute | solution.py:21
  77.8 16.1 %reduce-scatter.5.cloned.1.call-done = bf16[512,768]{0,1:T(8,128)(2,1)} async-done(((bf16[2048,768]{0,1:T(8,128)(2,1)}), bf16[512,768]{0,1:T(8,128)(2,1)}) %reduce-scatter.5.cloned.1.call-update) | async-done | bytes 786448 | tf_op jit(solution)/shard_map/reduce_scatter | solution.py:115
  106.7 7.8 %collective-permute-done.3 = bf16[2,255,256]{1,2,0:T(8,128)(2,1)} collective-permute-done((bf16[2,255,256]{1,2,0:T(8,128)(2,1)}, bf16[2,255,256]{1,2,0:T(8,128)(2,1)}, u32[]{:S(2)}, u32[]{:S(2)}) %collective-permute-start.3) | collective-permute-done | bytes 261152 | tf_op jit(solution)/shard_map/ppermute | solution.py:21
  124.9 21.4 %all-gather.8.cloned.1.call-done = bf16[4,512,256]{2,1,0:T(8,128)(2,1)} async-done(((bf16[1,512,256]{2,1,0:T(8,128)(2,1)}), bf16[4,512,256]{2,1,0:T(8,128)(2,1)}) %all-gather.8.cloned.1.call-update) | async-done | bytes 1048592 | tf_op jit(solution)/shard_map/all_gather | solution.py:120
  152.8 22.6 %reduce-scatter.7.cloned.1.call-done = bf16[128,1024]{1,0:T(8,128)(2,1)} async-done(((bf16[512,1024]{1,0:T(8,128)(2,1)}), bf16[128,1024]{1,0:T(8,128)(2,1)}) %reduce-scatter.7.cloned.1.call-update) | async-done | bytes 262160 | tf_op jit(solution)/shard_map/reduce_scatter | solution.py:123
  186.1 5.7 %psum.15 = f32[192]{0:T(256)S(1)} all-reduce(f32[192]{0:T(256)S(1)} %get-tuple-element.23), channel_id=1, replica_groups=mesh['req'=8,'row'=4,'col'=4] {'row'}, use_global_device_ids=true, to_apply=%region_9.10 | all-reduce | flops 192 | bytes 1536 | tf_op jit(solution)/shard_map/psum | solution.py:37
  204.5 6.6 %pad_maximum_fusion.1 = bf16[1024,4,3,256]{0,3,2,1:T(8,128)(2,1)} fusion(bf16[1024,4,1,256]{0,3,2,1:T(8,128)(2,1)} %bitcast.92, bf16[1024,4,1,256]{0,3,2,1:T(8,128)(2,1)} %bitcast.91, bf16[1024,4,1,256]{0,3,2,1:T(8,128)(2,1)} %bitcast.90), kind=kLoop, calls=%fused_computation.15 | loop fusion | flops 6291456 | bytes 12582912 | tf_op jit(solution)/shard_map/stack | solution.py:110
  211.2 12.1 %all-gather.10.cloned.1.call-done = bf16[768,1024]{1,0:T(8,128)(2,1)} async-done(((bf16[192,1024]{1,0:T(8,128)(2,1)}), bf16[768,1024]{1,0:T(8,128)(2,1)}) %all-gather.10.cloned.1.call-update) | async-done | bytes 1572880 | tf_op jit(solution)/shard_map/all_gather | solution.py:43
  223.3 9.1 %convolution_convert_fusion = bf16[4,768,768]{1,2,0:T(8,128)(2,1)} fusion(bf16[1024,4,768]{0,2,1:T(8,128)(2,1)} %bitcast.94, bf16[768,1024]{1,0:T(8,128)(2,1)} %all-gather.10.cloned.1.call-done), kind=kOutput, calls=%fused_computation.20 | convolution fusion | flops 4834197504 | bytes 12582912 | tf_op jit(solution)/shard_map/tf,frc->rtc/dot_general | solution.py:113
  232.4 6.6 %copy.53 = bf16[3072,768]{0,1:T(8,128)(2,1)} copy(bf16[3072,768]{1,0:T(8,128)(2,1)} %bitcast.95) | data formatting | bytes 9437184 | tf_op jit(solution)/shard_map/reshape | solution.py:114
  239.2 49.6 %reduce-scatter.9.cloned.1.call-done = bf16[768,768]{0,1:T(8,128)(2,1)} async-done(((bf16[3072,768]{0,1:T(8,128)(2,1)}), bf16[768,768]{0,1:T(8,128)(2,1)}) %reduce-scatter.9.cloned.1.call-update) | async-done | bytes 1179664 | tf_op jit(solution)/shard_map/reduce_scatter | solution.py:115
  291.1 5.7 %iota_compare_fusion = pred[768,6144]{1,0:T(8,128)(4,1)} fusion(s32[768]{0:T(1024)S(1)} %iota_add_fusion), kind=kLoop, calls=%fused_computation.12 | loop fusion | flops 4718592 | bytes 4721664 | tf_op jit(solution)/shard_map/ge | solution.py:206
  296.8 83.9 %all-gather.12.cloned.1.call-done = bf16[2,6144,256]{1,2,0:T(8,128)(2,1)} async-done(((bf16[2,768,256]{1,2,0:T(8,128)(2,1)}), bf16[2,6144,256]{1,2,0:T(8,128)(2,1)}) %all-gather.12.cloned.1.call-update) | async-done | bytes 6291472 | tf_op jit(solution)/shard_map/all_gather | solution.py:203
  380.7 5.4 %fusion.66 = (bf16[1,6144,256]{1,2,0:T(8,128)(2,1)S(1)}, bf16[1,6144,256]{1,2,0:T(8,128)(2,1)}) fusion(bf16[2,6144,256]{1,2,0:T(8,128)(2,1)} %all-gather.12.cloned.1.call-done), kind=kLoop, calls=%fused_computation.110 | loop fusion | bytes 12582912 | tf_op jit(solution)/shard_map/slice | solution.py:207
  386.1 14.7 %fusion.74 = f32[2,768,6144]{2,1,0:T(8,128)} fusion(bf16[768,2,128]{0,2,1:T(8,128)(2,1)S(1)} %bitcast.100, bf16[6144,2,128]{0,2,1:T(8,128)(2,1)S(1)} %bitcast.86), kind=kOutput, calls=%fused_computation.118 | convolution fusion | flops 2415919104 | bytes 41287680 | tf_op jit(solution)/shard_map/qhd,khd->hqk/dot_general | solution.py:62
  400.8 36.8 %fusion.73 = (f32[2,768]{1,0:T(2,128)S(1)}, bf16[2,768,6144]{2,1,0:T(8,128)(2,1)}) fusion(f32[2,768,6144]{2,1,0:T(8,128)} %fusion.74, pred[768,6144]{1,0:T(8,128)(4,1)S(1)} %bitcast.97), kind=kOutput, calls=%fused_computation.117 | output fusion | flops 75503616 | bytes 61347840 | tf_op jit(solution)/shard_map/sub | solution.py:67
  437.6 10.4 %fusion.32 = bf16[768,2,128]{0,2,1:T(8,128)(2,1)S(1)} fusion(bf16[6144,2,128]{0,2,1:T(8,128)(2,1)} %bitcast.99, bf16[2,768,6144]{2,1,0:T(8,128)(2,1)} %get-tuple-element.26, f32[768,2]{0,1:T(2,128)S(1)} %bitcast.111), kind=kOutput, calls=%fused_computation.38 | convolution fusion | flops 2416312320 | bytes 22419456 | tf_op jit(solution)/shard_map/hqk,khd->qhd/dot_general | solution.py:69
  449.0 22.7 %all-gather.14.cloned.1.call-done = bf16[4,768,256]{2,1,0:T(8,128)(2,1)} async-done(((bf16[1,768,256]{2,1,0:T(8,128)(2,1)}), bf16[4,768,256]{2,1,0:T(8,128)(2,1)}) %all-gather.14.cloned.1.call-update) | async-done | bytes 1572880 | tf_op jit(solution)/shard_map/all_gather | solution.py:120
  476.1 27.0 %reduce-scatter.11.cloned.1.call-done = bf16[192,1024]{1,0:T(8,128)(2,1)} async-done(((bf16[768,1024]{1,0:T(8,128)(2,1)}), bf16[192,1024]{1,0:T(8,128)(2,1)}) %reduce-scatter.11.cloned.1.call-update) | async-done | bytes 393232 | tf_op jit(solution)/shard_map/reduce_scatter | solution.py:123
  (99 shorter events, 89.8 us)
Async XLA Ops:
  6.5 465.2 %copy-start = (bf16[1024,1024]{1,0:T(8,128)(2,1)S(1)}, bf16[1024,1024]{1,0:T(8,128)(2,1)}, u32[]{:S(2)}) copy-start(bf16[1024,1024]{1,0:T(8,128)(2,1)} %param.27) | copy-start | bytes 6291460
  6.5 37.1 %all-gather.6.cloned.1.call-start = ((), (), s32[]{:S(2)}) async-start(), calls=%async_computation.4 | async-start | bytes 1310720 | tf_op jit(solution)/shard_map/all_gather | solution.py:43
  17.2 76.7 %reduce-scatter.5.cloned.1.call-start = ((), (), s32[]{:S(2)}) async-start(), calls=%async_computation.5 | async-start | bytes 3932160 | tf_op jit(solution)/shard_map/reduce_scatter | solution.py:115
  56.5 0.7 copy-start.3
  56.5 0.7 copy-start.4
  56.6 89.7 %all-gather.8.cloned.1.call-start = ((), (), s32[]{:S(2)}) async-start(), calls=%async_computation.6 | async-start | bytes 1310720 | tf_op jit(solution)/shard_map/all_gather | solution.py:120
  65.9 6.3 %collective-permute-start = (s32[2,255]{1,0:T(2,128)S(1)}, s32[2,255]{1,0:T(2,128)S(1)}, u32[]{:S(2)}, u32[]{:S(2)}) collective-permute-start(s32[2,255]{1,0:T(2,128)S(1)} %get-tuple-element.19), channel_id=1, source_target_pairs={{0,16},{16,32},{32,48},{48,64},{64,80},{80,96},{96,112},{1,17},{17... | collective-permute-start | bytes 6128 | tf_op jit(solution)/shard_map/ppermute | solution.py:19
  70.7 7.0 %collective-permute-start.1 = (s32[2,255]{1,0:T(2,128)S(1)}, s32[2,255]{1,0:T(2,128)S(1)}, u32[]{:S(2)}, u32[]{:S(2)}) collective-permute-start(s32[2,255]{1,0:T(2,128)S(1)} %get-tuple-element.20), channel_id=1, source_target_pairs={{16,0},{32,16},{48,32},{64,48},{80,64},{96,80},{112,96},{17,1},{33... | collective-permute-start | bytes 6128 | tf_op jit(solution)/shard_map/ppermute | solution.py:21
  96.0 10.8 %collective-permute-start.2 = (bf16[2,255,256]{1,2,0:T(8,128)(2,1)}, bf16[2,255,256]{1,2,0:T(8,128)(2,1)}, u32[]{:S(2)}, u32[]{:S(2)}) collective-permute-start(bf16[2,255,256]{1,2,0:T(8,128)(2,1)} %get-tuple-element.15), channel_id=1, source_target_pairs={{0,16},{16,32},{32,48},{48,64},{64,80},{80,96},{96,112},{1,17},{17... | collective-permute-start | bytes 783368 | tf_op jit(solution)/shard_map/ppermute | solution.py:19
  101.3 13.3 %collective-permute-start.3 = (bf16[2,255,256]{1,2,0:T(8,128)(2,1)}, bf16[2,255,256]{1,2,0:T(8,128)(2,1)}, u32[]{:S(2)}, u32[]{:S(2)}) collective-permute-start(bf16[2,255,256]{1,2,0:T(8,128)(2,1)} %get-tuple-element.16), channel_id=1, source_target_pairs={{16,0},{32,16},{48,32},{64,48},{80,64},{96,80},{112,96},{17,1},{33... | collective-permute-start | bytes 783368 | tf_op jit(solution)/shard_map/ppermute | solution.py:21
  124.8 50.5 %reduce-scatter.7.cloned.1.call-start = ((), (), s32[]{:S(2)}) async-start(), calls=%async_computation.7 | async-start | bytes 1310720 | tf_op jit(solution)/shard_map/reduce_scatter | solution.py:123
  146.3 4.3 copy-start.2
  146.3 29.1 %copy-start.1 = (bf16[128,1024]{1,0:T(8,128)(2,1)S(1)}, bf16[128,1024]{1,0:T(8,128)(2,1)}, u32[]{:S(2)}) copy-start(bf16[128,1024]{1,0:T(8,128)(2,1)} %param.15) | copy-start | bytes 786436
  150.5 72.8 %all-gather.10.cloned.1.call-start = ((), (), s32[]{:S(2)}) async-start(), calls=%async_computation.8 | async-start | bytes 1966080 | tf_op jit(solution)/shard_map/all_gather | solution.py:43
  176.4 8.3 %collective-permute-start.4 = (bf16[128,1024]{1,0:T(8,128)(2,1)S(1)}, bf16[128,1024]{1,0:T(8,128)(2,1)S(1)}, u32[]{:S(2)}, u32[]{:S(2)}) collective-permute-start(bf16[128,1024]{1,0:T(8,128)(2,1)S(1)} %fusion.39), channel_id=1, source_target_pairs={{1,0},{2,1},{3,2},{16,3},{17,16},{18,17},{19,18},{32,19},{33,32},{... | collective-permute-start | bytes 786440 | tf_op jit(solution)/shard_map/ppermute | solution.py:31
  192.6 96.1 %reduce-scatter.9.cloned.1.call-start = ((), (), s32[]{:S(2)}) async-start(), calls=%async_computation.9 | async-start | bytes 5898240 | tf_op jit(solution)/shard_map/reduce_scatter | solution.py:115
  239.1 141.6 %all-gather.12.cloned.1.call-start = ((), (), s32[]{:S(2)}) async-start(), calls=%async_computation.10 | async-start | bytes 7077888 | tf_op jit(solution)/shard_map/all_gather | solution.py:203
  291.1 180.7 %all-gather.14.cloned.1.call-start = ((), (), s32[]{:S(2)}) async-start(), calls=%async_computation.11 | async-start | bytes 1966080 | tf_op jit(solution)/shard_map/all_gather | solution.py:120
  380.7 20.1 %slice-start = ((s8[4718592]{0:T(1024)(128)(4,1)}), s8[4194304]{0:T(1024)(128)(4,1)S(1)}, s32[]{:S(2)}) async-start(s8[4718592]{0:T(1024)(128)(4,1)} %bitcast.96), calls=%async_computation.13 | async-start | bytes 8388608
  386.1 14.7 %slice-start.1 = ((s8[4718592]{0:T(1024)(128)(4,1)}), s8[524288]{0:T(1024)(128)(4,1)S(1)}, s32[]{:S(2)}) async-start(s8[4718592]{0:T(1024)(128)(4,1)} %bitcast.96), calls=%async_computation.14 | async-start | bytes 1048576
  449.0 54.2 %reduce-scatter.11.cloned.1.call-start = ((), (), s32[]{:S(2)}) async-start(), calls=%async_computation.12 | async-start | bytes 1966080 | tf_op jit(solution)/shard_map/reduce_scatter | solution.py:123
Sparse Core Ops, SparseCore 0:
  17.4 26.2 all-gather.5
  56.7 37.1 reduce-scatter.4
  124.9 21.2 all-gather.7
  150.6 24.6 reduce-scatter.6
  192.8 30.5 all-gather.9
  239.2 49.5 reduce-scatter.8
  291.4 89.2 all-gather.11
  449.1 22.6 all-gather.13
  476.3 26.8 reduce-scatter.10
where the time goes:
time: 513 us; the launch traced here: 512 us
  waiting for transfers between devices  283 us (55%)
  other arithmetic  67.9 us (13%)
  matrix products  59.4 us (12%)
  local copies, waits for them, and re-layouts  51.4 us (10%)
  blocking collectives  21.2 us (4%)
  starting transfers between devices  14.6 us (3%)
  between operations  13.5 us (3%)
    all_gather x1, waiting for transfers between devices, per_device(): piece = lax.all_gather(dec_pairs, 'req', axis=1, tiled=True)  83.9 us
    reduce_scatter x2, waiting for transfers between devices, head_project(): return lax.psum_scatter(summed, 'row', scatter_dimension=0, tiled=True)  65.7 us
    reduce_scatter x2, waiting for transfers between devices, out_project_heads(): lax.psum_scatter(summed.astype(jnp.bfloat16), 'col', scatter_dimension=0,...  49.6 us
    all_gather x2, waiting for transfers between devices, out_project_heads(): whole = lax.all_gather(attended, 'row', axis=0, tiled=False)  44.1 us
    sub x1, other arithmetic, attend_block(): weights = jnp.where(allowed[None], jnp.exp(scores - peak), 0.0)  36.8 us
    unnamed x20, local copies, waits for them, and re-layouts  24.3 us
    all_gather x2, waiting for transfers between devices, gather_cols(): return lax.all_gather(values, 'col', axis=0, tiled=True)  20.1 us
    dot_general x2, matrix products, head_project(): jnp.einsum('tf,frc->rtc', values, shaped, preferred_element_type=jnp.floa...  17.3 us
  transfers between devices with their start and end apart: 14, of which 13 were waited for; matrix products, arithmetic and copies ran while one was open for 10% of the time, Pallas kernels for 0%

commit v1 on v0

--- a/solution.py
+++ b/solution.py
@@ -200,7 +200,9 @@
     dec_proj = head_project(dec_cols, (dec_wq, dec_wk, dec_wv))
     dec_rows = dec_cols.shape[0]
     dec_pairs = jnp.stack([dec_proj[:, local : 2 * local], dec_proj[:, 2 * local :]])
-    piece = lax.all_gather(dec_pairs, "req", axis=1, tiled=True)
+    piece = jnp.concatenate(
+        lax.all_to_all(jnp.stack([dec_pairs] * lax.axis_size("req")), "req", 0, 0), axis=1
+    )
     token_slots = lax.axis_index("req") * dec_rows + jnp.arange(dec_rows, dtype=jnp.int32)
     all_slots = jnp.arange(piece.shape[1], dtype=jnp.int32)
     causal = token_slots[:, None] >= all_slots[None, :]

time: 513 us -> 528 us (1.029)
  local copies, waits for them, and re-layouts: 51.4 us -> 75.2 us
  waiting for transfers between devices: 283 us -> 267 us
  starting transfers between devices: 14.6 us -> 20.9 us
    all_gather x1 -> x0, waiting for transfers between devices: 83.9 us -> none  [per_device(): piece = lax.all_gather(dec_pairs, 'req', axis=1, tiled=True)]
    all_to_all x0 -> x1, waiting for transfers between devices: none -> 68.1 us  [per_device(): lax.all_to_all(jnp.stack([dec_pairs] * lax.axis_size('req')), 'req', 0, 0)]
    another operation x1 -> x4, local copies, waits for them, and re-layouts: 0.11 us -> 14.9 us  [the longest x2 11.5 us: split_heads(): return values.reshape(values.shape[0], values.shape[1] // HD, HD)]
    slice x2 -> x4, local copies, waits for them, and re-layouts: 6.71 us -> 15.8 us  [per_device(): dec_att = attend_block(dec_proj[:, :local], piece[0], piece[1], causal)]
    all_to_all x0 -> x1, starting transfers between devices: none -> 6.42 us  [per_device(): lax.all_to_all(jnp.stack([dec_pairs] * lax.axis_size('req')), 'req', 0, 0)]
    unnamed x20 -> x22, local copies, waits for them, and re-layouts: 24.3 us -> 24.3 us
  transfers between devices with their start and end apart: 14 -> 14, of which waited for: 13 -> 13; matrix products, arithmetic and copies ran while one was open for 10% -> 9% of each run, Pallas kernels for 0% -> 0%
where the time goes in v1:
time: 528 us; the launch traced here: 527 us
  waiting for transfers between devices  267 us (51%)
  local copies, waits for them, and re-layouts  75.2 us (14%)
  other arithmetic  67 us (13%)
  matrix products  61.3 us (12%)
  blocking collectives  21.2 us (4%)
  starting transfers between devices  20.9 us (4%)
  between operations  13.8 us (3%)
    all_to_all x1, waiting for transfers between devices, per_device(): lax.all_to_all(jnp.stack([dec_pairs] * lax.axis_size('req')), 'req', 0, 0)  68.1 us
    reduce_scatter x2, waiting for transfers between devices, head_project(): return lax.psum_scatter(summed, 'row', scatter_dimension=0, tiled=True)  65.8 us
    reduce_scatter x2, waiting for transfers between devices, out_project_heads(): lax.psum_scatter(summed.astype(jnp.bfloat16), 'col', scatter_dimension=0,...  49.6 us
    all_gather x2, waiting for transfers between devices, out_project_heads(): whole = lax.all_gather(attended, 'row', axis=0, tiled=False)  43.6 us
    sub x1, other arithmetic, attend_block(): weights = jnp.where(allowed[None], jnp.exp(scores - peak), 0.0)  36.8 us
    unnamed x22, local copies, waits for them, and re-layouts  24.3 us
    all_gather x2, waiting for transfers between devices, gather_cols(): return lax.all_gather(values, 'col', axis=0, tiled=True)  20.1 us
    dot_general x2, matrix products, head_project(): jnp.einsum('tf,frc->rtc', values, shaped, preferred_element_type=jnp.floa...  17.3 us
  transfers between devices with their start and end apart: 14, of which 13 were waited for; matrix products, arithmetic and copies ran while one was open for 9% of the time, Pallas kernels for 0%

profile of v1, /device:TPU:0, one launch (start us, length us, event | category | flops | bytes accessed | tf_op | source)
XLA Modules:
  0.0 526.7 jit_solution(11769364768176898750)
XLA Ops:
  7.8 7.0 %psum.14 = f32[128]{0:T(128)S(1)} all-reduce(f32[128]{0:T(128)S(1)} %fusion.36), channel_id=1, replica_groups=mesh['req'=8,'row'=4,'col'=4] {'row'}, use_global_device_ids=true, to_apply=%region_3.4 | all-reduce | flops 128 | bytes 1024 | tf_op jit(solution)/shard_map/psum | solution.py:37
  29.2 6.6 %pad_maximum_fusion = bf16[1024,4,3,256]{0,3,2,1:T(8,128)(2,1)} fusion(bf16[1024,4,1,256]{0,3,2,1:T(8,128)(2,1)} %bitcast.95, bf16[1024,4,1,256]{0,3,2,1:T(8,128)(2,1)} %bitcast.94, bf16[1024,4,1,256]{0,3,2,1:T(8,128)(2,1)} %bitcast.93), kind=kLoop, calls=%fused_computation.14 | loop fusion | flops 6291456 | bytes 12582912 | tf_op jit(solution)/shard_map/stack | solution.py:110
  35.7 7.9 %all-gather.5.cloned.1.call-done = bf16[512,1024]{1,0:T(8,128)(2,1)} async-done(((bf16[128,1024]{1,0:T(8,128)(2,1)}), bf16[512,1024]{1,0:T(8,128)(2,1)}) %all-gather.5.cloned.1.call-update) | async-done | bytes 1048592 | tf_op jit(solution)/shard_map/all_gather | solution.py:43
  43.7 8.2 %convolution_convert_fusion.1 = bf16[4,768,512]{1,2,0:T(8,128)(2,1)} fusion(bf16[1024,4,768]{0,2,1:T(8,128)(2,1)} %bitcast.99, bf16[512,1024]{1,0:T(8,128)(2,1)} %all-gather.5.cloned.1.call-done), kind=kOutput, calls=%fused_computation.21 | convolution fusion | flops 3222798336 | bytes 10485760 | tf_op jit(solution)/shard_map/tf,frc->rtc/dot_general | solution.py:113
  57.2 8.6 %all_gather.17 = s32[2,512]{1,0:T(2,128)S(1)} all-gather(s32[2,128]{1,0:T(2,128)S(1)} %pad_add_fusion.1), channel_id=1, replica_groups=mesh['req'=8,'row'=4,'col'=4] {'col'}, dimensions={1}, use_global_device_ids=true | all-gather | bytes 5120 | tf_op jit(solution)/shard_map/all_gather | solution.py:149
  77.8 16.1 %reduce-scatter.5.cloned.1.call-done = bf16[512,768]{0,1:T(8,128)(2,1)} async-done(((bf16[2048,768]{0,1:T(8,128)(2,1)}), bf16[512,768]{0,1:T(8,128)(2,1)}) %reduce-scatter.5.cloned.1.call-update) | async-done | bytes 786448 | tf_op jit(solution)/shard_map/reduce_scatter | solution.py:115
  106.7 7.8 %collective-permute-done.3 = bf16[2,255,256]{1,2,0:T(8,128)(2,1)} collective-permute-done((bf16[2,255,256]{1,2,0:T(8,128)(2,1)}, bf16[2,255,256]{1,2,0:T(8,128)(2,1)}, u32[]{:S(2)}, u32[]{:S(2)}) %collective-permute-start.3) | collective-permute-done | bytes 261152 | tf_op jit(solution)/shard_map/ppermute | solution.py:21
  124.9 21.4 %all-gather.7.cloned.1.call-done = bf16[4,512,256]{2,1,0:T(8,128)(2,1)} async-done(((bf16[1,512,256]{2,1,0:T(8,128)(2,1)}), bf16[4,512,256]{2,1,0:T(8,128)(2,1)}) %all-gather.7.cloned.1.call-update) | async-done | bytes 1048592 | tf_op jit(solution)/shard_map/all_gather | solution.py:120
  152.8 22.6 %reduce-scatter.7.cloned.1.call-done = bf16[128,1024]{1,0:T(8,128)(2,1)} async-done(((bf16[512,1024]{1,0:T(8,128)(2,1)}), bf16[128,1024]{1,0:T(8,128)(2,1)}) %reduce-scatter.7.cloned.1.call-update) | async-done | bytes 262160 | tf_op jit(solution)/shard_map/reduce_scatter | solution.py:123
  204.8 6.6 %pad_maximum_fusion.1 = bf16[1024,4,3,256]{0,3,2,1:T(8,128)(2,1)} fusion(bf16[1024,4,1,256]{0,3,2,1:T(8,128)(2,1)} %bitcast.98, bf16[1024,4,1,256]{0,3,2,1:T(8,128)(2,1)} %bitcast.97, bf16[1024,4,1,256]{0,3,2,1:T(8,128)(2,1)} %bitcast.96), kind=kLoop, calls=%fused_computation.15 | loop fusion | flops 6291456 | bytes 12582912 | tf_op jit(solution)/shard_map/stack | solution.py:110
  211.5 12.1 %all-gather.9.cloned.1.call-done = bf16[768,1024]{1,0:T(8,128)(2,1)} async-done(((bf16[192,1024]{1,0:T(8,128)(2,1)}), bf16[768,1024]{1,0:T(8,128)(2,1)}) %all-gather.9.cloned.1.call-update) | async-done | bytes 1572880 | tf_op jit(solution)/shard_map/all_gather | solution.py:43
  223.6 9.1 %convolution_convert_fusion = bf16[4,768,768]{1,2,0:T(8,128)(2,1)} fusion(bf16[1024,4,768]{0,2,1:T(8,128)(2,1)} %bitcast.100, bf16[768,1024]{1,0:T(8,128)(2,1)} %all-gather.9.cloned.1.call-done), kind=kOutput, calls=%fused_computation.20 | convolution fusion | flops 4834197504 | bytes 12582912 | tf_op jit(solution)/shard_map/tf,frc->rtc/dot_general | solution.py:113
  232.7 6.6 %copy.53 = bf16[3072,768]{0,1:T(8,128)(2,1)} copy(bf16[3072,768]{1,0:T(8,128)(2,1)} %bitcast.101) | data formatting | bytes 9437184 | tf_op jit(solution)/shard_map/reshape | solution.py:114
  239.4 49.7 %reduce-scatter.9.cloned.1.call-done = bf16[768,768]{0,1:T(8,128)(2,1)} async-done(((bf16[3072,768]{0,1:T(8,128)(2,1)}), bf16[768,768]{0,1:T(8,128)(2,1)}) %reduce-scatter.9.cloned.1.call-update) | async-done | bytes 1179664 | tf_op jit(solution)/shard_map/reduce_scatter | solution.py:115
  294.5 6.4 %all-to-all-start = ((bf16[8,2,768,256]{2,3,1,0:T(8,128)(2,1)}), bf16[8,2,768,256]{2,3,1,0:T(8,128)(2,1)}, u32[]{:S(2)}, u32[]{:S(2)}) async-start(bf16[8,2,768,256]{2,3,1,0:T(8,128)(2,1)} %stack.55), calls=%async_computation.3 | async-start | bytes 12582912 | tf_op jit(solution)/shard_map/all_to_all | solution.py:204
  300.9 5.7 %iota_compare_fusion = pred[768,6144]{1,0:T(8,128)(4,1)} fusion(s32[768]{0:T(1024)S(1)} %iota_add_fusion), kind=kLoop, calls=%fused_computation.12 | loop fusion | flops 4718592 | bytes 4721664 | tf_op jit(solution)/shard_map/ge | solution.py:208
  306.6 68.1 %all-to-all-done = bf16[8,2,768,256]{2,3,1,0:T(8,128)(2,1)} async-done(((bf16[8,2,768,256]{2,3,1,0:T(8,128)(2,1)}), bf16[8,2,768,256]{2,3,1,0:T(8,128)(2,1)}, u32[]{:S(2)}, u32[]{:S(2)}) %all-to-all-start) | async-done | bytes 6291488 | tf_op jit(solution)/shard_map/all_to_all | solution.py:204
  383.1 5.7 %reshape_squeeze.15 = bf16[6144,2,128]{0,2,1:T(8,128)(2,1)} reshape(bf16[1,8,768,256]{2,1,3,0:T(8,128)(2,1)} %copy.55) | data formatting | bytes 6291456 | tf_op jit(solution)/shard_map/reshape;squeeze | solution.py:57
  394.1 5.7 %reshape_squeeze.14 = bf16[6144,2,128]{0,2,1:T(8,128)(2,1)} reshape(bf16[1,8,768,256]{2,1,3,0:T(8,128)(2,1)} %copy.54) | data formatting | bytes 6291456 | tf_op jit(solution)/shard_map/reshape;squeeze | solution.py:57
  399.9 16.5 %fusion.74 = f32[2,768,6144]{2,1,0:T(8,128)} fusion(bf16[768,2,128]{0,2,1:T(8,128)(2,1)} %bitcast.105, bf16[6144,2,128]{0,2,1:T(8,128)(2,1)} %reshape_squeeze.15), kind=kOutput, calls=%fused_computation.118 | convolution fusion | flops 2415919104 | bytes 41287680 | tf_op jit(solution)/shard_map/qhd,khd->hqk/dot_general | solution.py:62
  416.3 36.8 %fusion.73 = (f32[2,768]{1,0:T(2,128)S(1)}, bf16[2,768,6144]{2,1,0:T(8,128)(2,1)}) fusion(f32[2,768,6144]{2,1,0:T(8,128)} %fusion.74, pred[768,6144]{1,0:T(8,128)(4,1)S(1)} %bitcast.103), kind=kOutput, calls=%fused_computation.117 | output fusion | flops 75503616 | bytes 61347840 | tf_op jit(solution)/shard_map/sub | solution.py:67
  453.1 10.4 %fusion.32 = bf16[768,2,128]{0,2,1:T(8,128)(2,1)S(1)} fusion(bf16[6144,2,128]{0,2,1:T(8,128)(2,1)} %reshape_squeeze.14, bf16[2,768,6144]{2,1,0:T(8,128)(2,1)} %get-tuple-element.26, f32[768,2]{0,1:T(2,128)S(1)} %bitcast.116), kind=kOutput, calls=%fused_computation.38 | convolution fusion | flops 2416312320 | bytes 22419456 | tf_op jit(solution)/shard_map/hqk,khd->qhd/dot_general | solution.py:69
  464.5 22.1 %all-gather.11.cloned.1.call-done = bf16[4,768,256]{2,1,0:T(8,128)(2,1)} async-done(((bf16[1,768,256]{2,1,0:T(8,128)(2,1)}), bf16[4,768,256]{2,1,0:T(8,128)(2,1)}) %all-gather.11.cloned.1.call-update) | async-done | bytes 1572880 | tf_op jit(solution)/shard_map/all_gather | solution.py:120
  491.1 27.0 %reduce-scatter.11.cloned.1.call-done = bf16[192,1024]{1,0:T(8,128)(2,1)} async-done(((bf16[768,1024]{1,0:T(8,128)(2,1)}), bf16[192,1024]{1,0:T(8,128)(2,1)}) %reduce-scatter.11.cloned.1.call-update) | async-done | bytes 393232 | tf_op jit(solution)/shard_map/reduce_scatter | solution.py:123
  (105 shorter events, 118.1 us)
Async XLA Ops:
  6.5 480.1 %copy-start = (bf16[1024,1024]{1,0:T(8,128)(2,1)S(1)}, bf16[1024,1024]{1,0:T(8,128)(2,1)}, u32[]{:S(2)}) copy-start(bf16[1024,1024]{1,0:T(8,128)(2,1)} %param.27) | copy-start | bytes 6291460
  6.5 37.1 %all-gather.5.cloned.1.call-start = ((), (), s32[]{:S(2)}) async-start(), calls=%async_computation.5 | async-start | bytes 1310720 | tf_op jit(solution)/shard_map/all_gather | solution.py:43
  17.2 76.7 %reduce-scatter.5.cloned.1.call-start = ((), (), s32[]{:S(2)}) async-start(), calls=%async_computation.6 | async-start | bytes 3932160 | tf_op jit(solution)/shard_map/reduce_scatter | solution.py:115
  56.5 0.7 copy-start.4
  56.5 0.7 copy-start.5
  56.6 89.7 %all-gather.7.cloned.1.call-start = ((), (), s32[]{:S(2)}) async-start(), calls=%async_computation.7 | async-start | bytes 1310720 | tf_op jit(solution)/shard_map/all_gather | solution.py:120
  65.9 6.3 %collective-permute-start = (s32[2,255]{1,0:T(2,128)S(1)}, s32[2,255]{1,0:T(2,128)S(1)}, u32[]{:S(2)}, u32[]{:S(2)}) collective-permute-start(s32[2,255]{1,0:T(2,128)S(1)} %get-tuple-element.19), channel_id=1, source_target_pairs={{0,16},{16,32},{32,48},{48,64},{64,80},{80,96},{96,112},{1,17},{17... | collective-permute-start | bytes 6128 | tf_op jit(solution)/shard_map/ppermute | solution.py:19
  70.7 7.0 %collective-permute-start.1 = (s32[2,255]{1,0:T(2,128)S(1)}, s32[2,255]{1,0:T(2,128)S(1)}, u32[]{:S(2)}, u32[]{:S(2)}) collective-permute-start(s32[2,255]{1,0:T(2,128)S(1)} %get-tuple-element.20), channel_id=1, source_target_pairs={{16,0},{32,16},{48,32},{64,48},{80,64},{96,80},{112,96},{17,1},{33... | collective-permute-start | bytes 6128 | tf_op jit(solution)/shard_map/ppermute | solution.py:21
  96.0 10.8 %collective-permute-start.2 = (bf16[2,255,256]{1,2,0:T(8,128)(2,1)}, bf16[2,255,256]{1,2,0:T(8,128)(2,1)}, u32[]{:S(2)}, u32[]{:S(2)}) collective-permute-start(bf16[2,255,256]{1,2,0:T(8,128)(2,1)} %get-tuple-element.15), channel_id=1, source_target_pairs={{0,16},{16,32},{32,48},{48,64},{64,80},{80,96},{96,112},{1,17},{17... | collective-permute-start | bytes 783368 | tf_op jit(solution)/shard_map/ppermute | solution.py:19
  101.3 13.3 %collective-permute-start.3 = (bf16[2,255,256]{1,2,0:T(8,128)(2,1)}, bf16[2,255,256]{1,2,0:T(8,128)(2,1)}, u32[]{:S(2)}, u32[]{:S(2)}) collective-permute-start(bf16[2,255,256]{1,2,0:T(8,128)(2,1)} %get-tuple-element.16), channel_id=1, source_target_pairs={{16,0},{32,16},{48,32},{64,48},{80,64},{96,80},{112,96},{17,1},{33... | collective-permute-start | bytes 783368 | tf_op jit(solution)/shard_map/ppermute | solution.py:21
  124.8 50.5 %reduce-scatter.7.cloned.1.call-start = ((), (), s32[]{:S(2)}) async-start(), calls=%async_computation.8 | async-start | bytes 1310720 | tf_op jit(solution)/shard_map/reduce_scatter | solution.py:123
  146.3 4.3 copy-start.3
  146.3 29.1 %copy-start.1 = (bf16[128,1024]{1,0:T(8,128)(2,1)S(1)}, bf16[128,1024]{1,0:T(8,128)(2,1)}, u32[]{:S(2)}) copy-start(bf16[128,1024]{1,0:T(8,128)(2,1)} %param.15) | copy-start | bytes 786436
  150.5 73.1 %all-gather.9.cloned.1.call-start = ((), (), s32[]{:S(2)}) async-start(), calls=%async_computation.9 | async-start | bytes 1966080 | tf_op jit(solution)/shard_map/all_gather | solution.py:43
  176.4 2.9 copy-start.2
  176.4 8.4 %collective-permute-start.4 = (bf16[128,1024]{1,0:T(8,128)(2,1)S(1)}, bf16[128,1024]{1,0:T(8,128)(2,1)}, u32[]{:S(2)}, u32[]{:S(2)}) collective-permute-start(bf16[128,1024]{1,0:T(8,128)(2,1)S(1)} %fusion.39), channel_id=1, source_target_pairs={{1,0},{2,1},{3,2},{16,3},{17,16},{18,17},{19,18},{32,19},{33,32},{... | collective-permute-start | bytes 786440 | tf_op jit(solution)/shard_map/ppermute | solution.py:31
  192.9 96.1 %reduce-scatter.9.cloned.1.call-start = ((), (), s32[]{:S(2)}) async-start(), calls=%async_computation.10 | async-start | bytes 5898240 | tf_op jit(solution)/shard_map/reduce_scatter | solution.py:115
  294.5 80.2 %all-to-all-start = ((bf16[8,2,768,256]{2,3,1,0:T(8,128)(2,1)}), bf16[8,2,768,256]{2,3,1,0:T(8,128)(2,1)}, u32[]{:S(2)}, u32[]{:S(2)}) async-start(bf16[8,2,768,256]{2,3,1,0:T(8,128)(2,1)} %stack.55), calls=%async_computation.3 | async-start | bytes 12582912 | tf_op jit(solution)/shard_map/all_to_all | solution.py:204
  300.9 185.8 %all-gather.11.cloned.1.call-start = ((), (), s32[]{:S(2)}) async-start(), calls=%async_computation.11 | async-start | bytes 1966080 | tf_op jit(solution)/shard_map/all_gather | solution.py:120
  394.1 22.2 %slice-start = ((s8[4718592]{0:T(1024)(128)(4,1)}), s8[524288]{0:T(1024)(128)(4,1)S(1)}, s32[]{:S(2)}) async-start(s8[4718592]{0:T(1024)(128)(4,1)} %bitcast.102), calls=%async_computation.13 | async-start | bytes 1048576
  399.9 16.5 %slice-start.1 = ((s8[4718592]{0:T(1024)(128)(4,1)}), s8[4194304]{0:T(1024)(128)(4,1)S(1)}, s32[]{:S(2)}) async-start(s8[4718592]{0:T(1024)(128)(4,1)} %bitcast.102), calls=%async_computation.14 | async-start | bytes 8388608
  464.5 53.6 %reduce-scatter.11.cloned.1.call-start = ((), (), s32[]{:S(2)}) async-start(), calls=%async_computation.12 | async-start | bytes 1966080 | tf_op jit(solution)/shard_map/reduce_scatter | solution.py:123
Sparse Core Ops, SparseCore 0:
  17.4 26.2 all-gather.4
  56.7 37.1 reduce-scatter.4
  124.9 21.2 all-gather.6
  150.6 24.6 reduce-scatter.6
  193.0 30.5 all-gather.8
  239.5 49.5 reduce-scatter.8
  464.6 22.0 all-gather.10
  491.2 26.8 reduce-scatter.10
